TPU v7x, 32 devices: a whole 2x2x4 slice. The times are simulated.
32 devices in a mesh: groups: 2 (over x), chan: 16 (over z, y, core), freq: 1.
Axes of the slice: x: 2, y: 2, z: 4, core: 2. Of those that a mesh axis runs over, the one named last changes fastest.
Arguments:
- raw: bfloat16 [256, 16, 12000], P(('groups', 'chan'), 'freq'), parts along dimension 0, may hold values from -100 to 100, as said below
- lengths: int32 [256, 16], P(('groups', 'chan'), 'freq'), parts along dimension 0, may hold values from 6000 to 12000
- quality: int32 [256], P('groups'), parts along dimension 0, may hold values 0 or 1
- assignment: int32 [256], P('groups'), parts along dimension 0, may hold values from 0 to 127, as said below
Outputs:
- cross: bfloat16 [512, 256, 2, 128], P('freq', ('groups', 'chan')), parts along dimension 1
There are 2 independent parts, one for each index of `groups`. A program takes and returns all parts, laid end to end along the dimension named above; each array names one. Nothing has to cross between parts.
Inputs may be any that keep to these rules, and one draw needn't show every extreme that they name: `raw`: records are clipped to this range. `assignment`: A permutation. The 8 channels of one file block (consecutive entries) land at most 1 in any one block of 8 consecutive positions, and some pair of blocks reaches 1.
All inputs are finite; a program needn't handle non-finite values.
Results may differ from a plain program's by a relative error of at most 0.012.
The roundings to bfloat16 on the way count: a program that leaves them out, or rounds other values in their place, can miss the bound.
Values may be sent and summed in bfloat16 or wider, within the bound.
No kernel may reach another device: no remote copies, remote signals or barrier semaphores. Data moves between devices by JAX's collectives and lax.ppermute only.
A program may use at most 128 MiB of HBM per device.

v0:
```python
import math

import jax
import jax.numpy as jnp
from jax import lax
from jax.sharding import PartitionSpec as P

WIN = 12000
NB = 512
K0 = 6
SUB = 32


def dft_table(first_sample, sample_count):
    samples = first_sample + jnp.arange(sample_count, dtype=jnp.int32)
    bin_index = K0 + jnp.arange(NB, dtype=jnp.int32)
    residue = samples[:, None] * bin_index[None, :] % WIN
    angles = residue.astype(jnp.float32) * (2.0 * math.pi / WIN)
    return jnp.concatenate([jnp.cos(angles), -jnp.sin(angles)], axis=1).astype(jnp.bfloat16)


def prepare(raw_block, valid_lengths):
    positions = jnp.arange(WIN, dtype=jnp.int32)
    inside = positions[None, None, :] < valid_lengths[:, :, None]
    values = raw_block.astype(jnp.float32)
    kept = jnp.where(inside, values, 0.0)
    average = jnp.sum(kept, axis=-1) / valid_lengths.astype(jnp.float32)
    taper = 0.5 - 0.5 * jnp.cos(positions.astype(jnp.float32) * (2.0 * math.pi / WIN))
    return jnp.where(inside, (values - average[:, :, None]) * taper[None, None, :], 0.0).astype(
        jnp.bfloat16
    )


def whiten(spectra):
    row_count = spectra.shape[0]
    grouped = spectra.reshape(row_count, 2, NB // SUB, SUB)
    power = jnp.sum(grouped * grouped, axis=(1, 3)) / SUB
    factor = lax.rsqrt(power + 1e-06)
    return (grouped * factor[:, None, :, None]).reshape(row_count, 2, NB).astype(jnp.bfloat16)


def spectra_of(shaped_rows):
    row_count = shaped_rows.shape[0]
    pieces = 8
    block_width = WIN // pieces
    total = jnp.zeros((row_count, 2 * NB), jnp.float32)
    for block_index in range(pieces):
        first_sample = block_index * block_width
        segment = lax.slice_in_dim(shaped_rows, first_sample, first_sample + block_width, axis=1)
        total = total + jnp.dot(
            segment, dft_table(first_sample, block_width), preferred_element_type=jnp.float32
        )
    return whiten(total)


def cross_block(left_rows, right_rows, all_windows):
    bins_here = left_rows.shape[3]
    left_side = left_rows.transpose(3, 0, 2, 1).reshape(
        bins_here, left_rows.shape[0], 2 * all_windows
    )
    right_count = right_rows.shape[0]
    right_plain = right_rows.transpose(3, 2, 1, 0).reshape(bins_here, 2 * all_windows, right_count)
    turned = jnp.stack([-right_rows[:, :, 1], right_rows[:, :, 0]], axis=2)
    right_turned = turned.transpose(3, 2, 1, 0).reshape(bins_here, 2 * all_windows, right_count)
    real_part = jnp.einsum(
        "bik,bkj->bij", left_side, right_plain, preferred_element_type=jnp.float32
    )
    imag_part = jnp.einsum(
        "bik,bkj->bij", left_side, right_turned, preferred_element_type=jnp.float32
    )
    return (jnp.stack([real_part, imag_part], axis=2) / all_windows).astype(jnp.bfloat16)


def body(raw, lengths, quality, assignment):
    channel_count = lax.axis_size("chan")
    my_index = lax.axis_index("chan")
    block_rows, window_count, sample_count = raw.shape
    capacity = max(1, block_rows // channel_count)
    total_channels = assignment.shape[0]
    targets_all = assignment.reshape(channel_count, block_rows) // block_rows
    row_numbers = jnp.arange(block_rows, dtype=jnp.int32)
    same_target = targets_all[:, :, None] == targets_all[:, None, :]
    earlier = row_numbers[None, None, :] < row_numbers[None, :, None]
    slot_table = jnp.sum(jnp.logical_and(same_target, earlier), axis=2)
    quality_table = quality.reshape(channel_count, block_rows)
    my_targets = lax.dynamic_index_in_dim(targets_all, my_index, 0, keepdims=False)
    my_slots = lax.dynamic_index_in_dim(slot_table, my_index, 0, keepdims=False)
    my_quality = lax.dynamic_index_in_dim(quality_table, my_index, 0, keepdims=False)
    device_numbers = jnp.arange(channel_count, dtype=jnp.int32)
    slot_numbers = jnp.arange(capacity, dtype=jnp.int32)
    match_table = jnp.logical_and(
        jnp.logical_and(
            my_targets[None, None, :] == device_numbers[:, None, None],
            my_slots[None, None, :] == slot_numbers[None, :, None],
        ),
        my_quality[None, None, :] == 1,
    )
    present = jnp.any(match_table, axis=2).reshape(-1)
    source_row = jnp.sum(jnp.where(match_table, row_numbers[None, None, :], 0), axis=2).reshape(-1)
    inverse = (
        jnp.zeros((total_channels,), jnp.int32)
        .at[assignment]
        .set(jnp.arange(total_channels, dtype=jnp.int32))
    )
    arrivals = lax.dynamic_slice_in_dim(inverse, my_index * block_rows, block_rows)
    source_device = arrivals // block_rows
    flat_slot = source_device * capacity + jnp.take(slot_table.reshape(-1), arrivals)
    arrival_good = jnp.take(quality, arrivals)
    shaped = prepare(raw, lengths)
    picked = jnp.take(shaped, source_row, axis=0)
    kept_rows = picked * present.astype(shaped.dtype).reshape((-1,) + (1,) * (shaped.ndim - 1))
    arrived = lax.all_to_all(
        kept_rows.reshape((channel_count, capacity) + shaped.shape[1:]),
        "chan",
        split_axis=0,
        concat_axis=0,
        tiled=True,
    )
    flat_rows = arrived.reshape((channel_count * capacity,) + arrived.shape[2:])
    picked = jnp.take(flat_rows, flat_slot, axis=0)
    local_rows = picked * arrival_good.astype(arrived.dtype).reshape(
        (-1,) + (1,) * (arrived.ndim - 2)
    )
    whitened = spectra_of(local_rows.reshape(block_rows * window_count, sample_count)).reshape(
        block_rows, window_count, 2, NB
    )
    panel = lax.all_to_all(whitened, "freq", split_axis=3, concat_axis=1, tiled=True)
    all_windows = panel.shape[1]
    return cross_block(panel, lax.all_gather(panel, "chan", axis=0, tiled=True), all_windows)


def solution(mesh):
    return jax.shard_map(
        body,
        mesh=mesh,
        in_specs=(
            P(("groups", "chan"), "freq", None),
            P(("groups", "chan"), "freq"),
            P("groups"),
            P("groups"),
        ),
        out_specs=P("freq", ("groups", "chan"), None, None),
        check_vma=False,
    )
```

profile of v0, /device:TPU:0, one launch (start us, length us, event | category | flops | bytes accessed | tf_op | source)
XLA Modules:
  0.0 277.0 jit_solution(14290823064365634316)
XLA Ops:
  8.8 3.3 %fusion = f32[8,16]{1,0:T(8,128)S(1)} fusion(bf16[8,16,12000]{2,1,0:T(8,128)(2,1)} %param.6, s32[8,16]{1,0:T(8,128)} %param.7), kind=kLoop, calls=%fused_computation.7 | loop fusion | flops 6143872 | bytes 3073024 | tf_op jit(solution)/shard_map/reduce_sum | solution.py:27
  12.1 1.5 fusion.3
  13.6 3.5 %gather_fusion = bf16[16,16,12000]{2,1,0:T(8,128)(2,1)} fusion(bf16[8,16,12000]{2,1,0:T(8,128)(2,1)S(1)} %fusion.3, s32[1024]{0:T(1024)S(1)} %pad_clamp_fusion.1), kind=kCustom, calls=%fused_computation.2 | custom fusion | bytes 12288064 | tf_op jit(solution)/shard_map/jit(_take)/gather | solution.py:110
  17.2 6.0 %fusion.4 = bf16[16,1,16,12000]{3,2,1,0:T(8,128)(2,1)} fusion(bf16[16,16,12000]{2,1,0:T(8,128)(2,1)} %gather_fusion, pred[16]{0:T(512)(128)(4,1)S(1)} %compare_and_fusion.1, bf16[16]{0:T(256)(128)(2,1)S(1)} %convert_element_type.89), kind=kLoop, calls=%fused_computation.12 | loop fusion | flops 6144000 | bytes 12288048 | tf_op jit(solution)/shard_map/mul | solution.py:111
  23.1 7.6 %all-to-all-start = ((bf16[16,1,16,12000]{3,2,1,0:T(8,128)(2,1)}), bf16[16,1,16,12000]{3,2,1,0:T(8,128)(2,1)}, u32[]{:S(2)}, u32[]{:S(2)}) async-start(bf16[16,1,16,12000]{3,2,1,0:T(8,128)(2,1)} %fusion.4), calls=%async_computation | async-start | bytes 12320768 | tf_op jit(solution)/shard_map/all_to_all | solution.py:112
  30.9 1.2 scatter_custom_fusion
  34.1 109.5 %cosine_convert_fusion = (bf16[1500,512]{1,0:T(8,128)(2,1)}, bf16[1500,512]{1,0:T(8,128)(2,1)}, bf16[1500,512]{1,0:T(8,128)(2,1)}, bf16[1500,512]{1,0:T(8,128)(2...) fusion(s32[1500]{0:T(1024)S(1)} %get-tuple-element.40, ...), kind=kLoop, calls=%fused_computation.76 | loop fusion | flops 73728000 | bytes 24620048 | tf_op jit(solution)/shard_map/convert
  143.6 3.5 %gather_fusion.1 = bf16[8,16,12000]{2,1,0:T(8,128)(2,1)S(1)} fusion(bf16[16,16,12000]{2,1,0:T(8,128)(2,1)} %bitcast.5, s32[1024]{0:T(1024)S(1)} %pad_clamp_fusion), kind=kCustom, calls=%fused_computation.3 | custom fusion | bytes 6144032 | tf_op jit(solution)/shard_map/jit(_take)/gather | solution.py:120
  147.6 0.9 copy-done.17
  149.5 0.8 copy-done.15
  153.3 0.8 copy-done.11
  155.2 0.8 copy-done.9
  158.9 0.8 copy-done.5
  160.8 0.8 copy-done.3
  164.2 0.8 fusion.100
  165.0 1.7 copy.42
  166.8 70.6 %all-gather.2.cloned.1.call-done = bf16[128,16,2,512]{3,1,2,0:T(8,128)(2,1)} async-done(((bf16[8,16,2,512]{3,1,2,0:T(8,128)(2,1)}), bf16[128,16,2,512]{3,1,2,0:T(8,128)(2,1)}) %all-gather.2.cloned.1.call-update) | async-done | bytes 4194320 | tf_op jit(solution)/shard_map/all_gather | solution.py:129
  237.4 9.1 %copy.41 = bf16[512,2,16,128]{3,2,1,0:T(8,128)(2,1)} copy(bf16[512,2,16,128]{0,2,1,3:T(8,128)(2,1)} %bitcast.37) | data formatting | bytes 8388608 | tf_op jit(solution)/shard_map/transpose | solution.py:62
  246.5 2.5 slice_negate_fusion
  249.0 2.3 maximum_bitcast_fusion
  251.3 9.1 %copy.43 = bf16[512,2,16,128]{3,2,1,0:T(8,128)(2,1)} copy(bf16[512,2,16,128]{0,2,1,3:T(8,128)(2,1)} %maximum_bitcast_fusion) | data formatting | bytes 8388608 | tf_op jit(solution)/shard_map/transpose | solution.py:64
  260.5 3.5 %convolution_bitcast_fusion.1 = f32[512,8,1,128]{3,1,0,2:T(8,128)S(1)} fusion(bf16[512,8,32]{2,1,0:T(8,128)(2,1)S(1)} %copy.42, bf16[512,32,128]{2,1,0:T(8,128)(2,1)} %bitcast.35), kind=kOutput, calls=%fused_computation.125 | convolution fusion | flops 33554432 | bytes 6553600 | tf_op jit(solution)/shard_map/bik,bkj->bij/dot_general | solution.py:65
  264.0 1.3 convolution_bitcast_fusion
  265.6 4.6 %copy.45 = bf16[512,8,2,128]{3,2,1,0:T(2,128)(2,1)} copy(bf16[512,8,2,128]{3,1,0,2:T(8,128)(2,1)S(1)} %fusion.5) | data formatting | bytes 4194304 | tf_op jit(solution)/shard_map/convert_element_type | solution.py:71
  (93 shorter events, 17.0 us)
Async XLA Ops:
  6.5 5.5 %copy-start.19 = (s32[8,16]{1,0:T(8,128)S(1)}, s32[8,16]{1,0:T(8,128)}, u32[]{:S(2)}) copy-start(s32[8,16]{1,0:T(8,128)} %param.7) | copy-start | bytes 1540
  8.1 4.0 %copy-start.2 = (bf16[8,16,12000]{2,1,0:T(8,128)(2,1)S(1)}, bf16[8,16,12000]{2,1,0:T(8,128)(2,1)}, u32[]{:S(2)}) copy-start(bf16[8,16,12000]{2,1,0:T(8,128)(2,1)} %param.6) | copy-start | bytes 9216004
  23.1 7.7 %copy-start.20 = (s32[128]{0:T(128)S(1)}, s32[128]{0:T(128)}, u32[]{:S(2)}) copy-start(s32[128]{0:T(128)} %param.9) | copy-start | bytes 1540
  23.1 9.0 %copy-start = (s32[128]{0:T(128)S(1)}, s32[128]{0:T(128)}, u32[]{:S(2)}) copy-start(s32[128]{0:T(128)} %param.8) | copy-start | bytes 1540
  23.1 120.5 %all-to-all-start = ((bf16[16,1,16,12000]{3,2,1,0:T(8,128)(2,1)}), bf16[16,1,16,12000]{3,2,1,0:T(8,128)(2,1)}, u32[]{:S(2)}, u32[]{:S(2)}) async-start(bf16[16,1,16,12000]{3,2,1,0:T(8,128)(2,1)} %fusion.4), calls=%async_computation | async-start | bytes 12320768 | tf_op jit(solution)/shard_map/all_to_all | solution.py:112
  30.7 206.6 %all-gather.2.cloned.1.call-start = ((), (), s32[]{:S(2)}) async-start(), calls=%async_computation.1 | async-start | bytes 4456448 | tf_op jit(solution)/shard_map/all_gather | solution.py:129
  147.1 1.4 copy-start.17
  147.1 1.9 copy-start.18
  149.0 1.4 copy-start.15
  149.0 1.9 copy-start.16
  150.8 1.4 copy-start.13
  150.8 1.9 copy-start.14
  152.7 1.4 copy-start.11
  152.7 1.9 copy-start.12
  154.5 1.4 copy-start.9
  154.5 1.9 copy-start.10
  156.4 1.4 copy-start.7
  156.4 1.9 copy-start.8
  158.3 1.4 copy-start.5
  158.3 1.9 copy-start.6
  160.1 1.4 copy-start.3
  160.1 1.9 copy-start.4
  260.5 3.5 %copy-start.1 = (bf16[512,2,16,128]{3,2,1,0:T(8,128)(2,1)S(1)}, bf16[512,2,16,128]{3,2,1,0:T(8,128)(2,1)}, u32[]{:S(2)}) copy-start(bf16[512,2,16,128]{3,2,1,0:T(8,128)(2,1)} %copy.43) | copy-start | bytes 12582916
Sparse Core Ops, SparseCore 0:
  165.1 72.1 all-gather.1
where the time goes:
time: 278 us; the launch traced here: 277 us
  other arithmetic  128 us (46%)
  waiting for transfers between devices  70.6 us (25%)
  local copies, waits for them, and re-layouts  47.6 us (17%)
  between operations  13.7 us (5%)
  matrix products  9.73 us (4%)
  starting transfers between devices  7.63 us (3%)
    another operation x1, other arithmetic  110 us
    all_gather x1, waiting for transfers between devices, body(): lax.all_gather(panel, 'chan', axis=0, tiled=True)  70.6 us
    unnamed x42, local copies, waits for them, and re-layouts  10 us
    transpose x1, local copies, waits for them, and re-layouts, cross_block(): turned.transpose(3, 2, 1, 0)  9.15 us
    transpose x1, local copies, waits for them, and re-layouts, cross_block(): right_rows.transpose(3, 2, 1, 0)  9.12 us
    all_to_all x1, starting transfers between devices, body(): lax.all_to_all(kept_rows.reshape((channel_count, capacity) + shaped.shape...  7.59 us
    mul x1, other arithmetic, body(): picked * present.astype(shaped.dtype).reshape((-1,) + (1,) * (shaped.ndim...  5.97 us
  transfers between devices with their start and end apart: 2, of which 1 were waited for; matrix products, arithmetic and copies ran while one was open for 41% of the time, Pallas kernels for 0%

commit v1 on v0

v1 whole, which is shorter than its diff:
```python
import math

import jax
import jax.numpy as jnp
from jax import lax
from jax.sharding import PartitionSpec as P

WIN = 12000
NB = 512
K0 = 6
SUB = 32
SPLIT = 100


def small_table(sample_values):
    bin_index = K0 + jnp.arange(NB, dtype=jnp.int32)
    residue = sample_values[:, None] * bin_index[None, :] % WIN
    angles = residue.astype(jnp.float32) * (2.0 * math.pi / WIN)
    return jnp.cos(angles), jnp.sin(angles)


def dft_table():
    high = jnp.arange(WIN // SPLIT, dtype=jnp.int32) * SPLIT
    low = jnp.arange(SPLIT, dtype=jnp.int32)
    cos_high, sin_high = small_table(high)
    cos_low, sin_low = small_table(low)
    cos_all = cos_high[:, None, :] * cos_low[None, :, :] - sin_high[:, None, :] * sin_low[None, :, :]
    sin_all = sin_high[:, None, :] * cos_low[None, :, :] + cos_high[:, None, :] * sin_low[None, :, :]
    table = jnp.concatenate([cos_all, -sin_all], axis=2).astype(jnp.bfloat16)
    return table.reshape(WIN, 2 * NB)


def prepare(raw_block, valid_lengths):
    positions = jnp.arange(WIN, dtype=jnp.int32)
    inside = positions[None, None, :] < valid_lengths[:, :, None]
    values = raw_block.astype(jnp.float32)
    kept = jnp.where(inside, values, 0.0)
    average = jnp.sum(kept, axis=-1) / valid_lengths.astype(jnp.float32)
    taper = 0.5 - 0.5 * jnp.cos(positions.astype(jnp.float32) * (2.0 * math.pi / WIN))
    return jnp.where(inside, (values - average[:, :, None]) * taper[None, None, :], 0.0).astype(
        jnp.bfloat16
    )


def whiten(spectra):
    row_count = spectra.shape[0]
    grouped = spectra.reshape(row_count, 2, NB // SUB, SUB)
    power = jnp.sum(grouped * grouped, axis=(1, 3)) / SUB
    factor = lax.rsqrt(power + 1e-06)
    return (grouped * factor[:, None, :, None]).reshape(row_count, 2, NB).astype(jnp.bfloat16)


def body(raw, lengths, quality, assignment):
    my_index = lax.axis_index("chan")
    block_rows, window_count, sample_count = raw.shape
    total_channels = assignment.shape[0]
    shaped = prepare(raw, lengths)
    spectra = jnp.dot(
        shaped.reshape(block_rows * window_count, sample_count),
        dft_table(),
        preferred_element_type=jnp.float32,
    )
    whitened = whiten(spectra).reshape(block_rows, window_count, 2, NB)
    my_quality = lax.dynamic_slice_in_dim(quality, my_index * block_rows, block_rows)
    whitened = whitened * my_quality.astype(jnp.bfloat16)[:, None, None, None]
    panel = lax.all_to_all(whitened, "freq", split_axis=3, concat_axis=1, tiled=True)
    all_windows = panel.shape[1]
    bins_here = panel.shape[3]
    gathered = lax.all_gather(panel, "chan", axis=0, tiled=True)
    inverse = (
        jnp.zeros((total_channels,), jnp.int32)
        .at[assignment]
        .set(jnp.arange(total_channels, dtype=jnp.int32))
    )
    ordered = jnp.take(gathered, inverse, axis=0)
    mine = lax.dynamic_slice_in_dim(inverse, my_index * block_rows, block_rows)
    left = jnp.take(gathered, mine, axis=0)
    left_re = left[:, :, 0, :]
    left_im = left[:, :, 1, :]
    plain = jnp.stack([left_re, left_im], axis=1)
    turned = jnp.stack([left_im, -left_re], axis=1)
    left_rows = jnp.stack([plain, turned], axis=1)
    left_rows = left_rows.transpose(4, 0, 1, 2, 3).reshape(bins_here, block_rows * 2, 2 * all_windows)
    right = ordered.transpose(3, 2, 1, 0).reshape(bins_here, 2 * all_windows, total_channels)
    out = jnp.einsum("bik,bkj->bij", left_rows, right, preferred_element_type=jnp.float32)
    return (out / all_windows).astype(jnp.bfloat16).reshape(bins_here, block_rows, 2, total_channels)


def solution(mesh):
    return jax.shard_map(
        body,
        mesh=mesh,
        in_specs=(
            P(("groups", "chan"), "freq", None),
            P(("groups", "chan"), "freq"),
            P("groups"),
            P("groups"),
        ),
        out_specs=P("freq", ("groups", "chan"), None, None),
        check_vma=False,
    )
```

time: 278 us -> 214 us (0.77)
  other arithmetic: 128 us -> 42.8 us
  local copies, waits for them, and re-layouts: 47.6 us -> 87.4 us
  waiting for transfers between devices: 70.6 us -> 51.9 us
  starting transfers between devices: 7.63 us -> 0.01 us
  matrix products: 9.73 us -> 16.1 us
    another operation x1 -> x2, other arithmetic: 110 us -> 12.4 us
    dot_general x0 -> x1, local copies, waits for them, and re-layouts: none -> 32.7 us  [body(): jnp.dot(shaped.reshape(block_rows * window_count, sample_count), dft_tabl...]
    dot_general x0 -> x1, other arithmetic: none -> 20.5 us  [body(): jnp.dot(shaped.reshape(block_rows * window_count, sample_count), dft_tabl...]
    all_gather x1, waiting for transfers between devices: 70.6 us -> 51.9 us  [body(): gathered = lax.all_gather(panel, 'chan', axis=0, tiled=True)]
    transpose x2 -> x1, local copies, waits for them, and re-layouts: 18.3 us -> 0.04 us  [body(): left_rows.transpose(4, 0, 1, 2, 3)]
    neg x0 -> x1, local copies, waits for them, and re-layouts: none -> 16.1 us  [dft_table(): table = jnp.concatenate([cos_all, -sin_all], axis=2).astype(jnp.bfloat16)]
    sub x0 -> x1, local copies, waits for them, and re-layouts: none -> 16.1 us  [dft_table(): cos_high[:, None, :] * cos_low[None, :, :]]
    unnamed x42 -> x8, local copies, waits for them, and re-layouts: 10 us -> 0.02 us
  transfers between devices with their start and end apart: 2 -> 1, of which waited for: 1 -> 1; matrix products, arithmetic and copies ran while one was open for 41% -> 1% of each run, Pallas kernels for 0% -> 0%
where the time goes in v1:
time: 214 us; the launch traced here: 212 us
  local copies, waits for them, and re-layouts  87.4 us (41%)
  waiting for transfers between devices  51.9 us (24%)
  other arithmetic  42.8 us (20%)
  matrix products  16.1 us (8%)
  between operations  13.6 us (6%)
    all_gather x1, waiting for transfers between devices, body(): gathered = lax.all_gather(panel, 'chan', axis=0, tiled=True)  51.9 us
    dot_general x1, local copies, waits for them, and re-layouts, body(): jnp.dot(shaped.reshape(block_rows * window_count, sample_count), dft_tabl...  32.7 us
    dot_general x1, other arithmetic, body(): jnp.dot(shaped.reshape(block_rows * window_count, sample_count), dft_tabl...  20.5 us
    neg x1, local copies, waits for them, and re-layouts, dft_table(): table = jnp.concatenate([cos_all, -sin_all], axis=2).astype(jnp.bfloat16)  16.1 us
    sub x1, local copies, waits for them, and re-layouts, dft_table(): cos_high[:, None, :] * cos_low[None, :, :]  16.1 us
    another operation x1, other arithmetic  12.4 us
    dot_general x1, matrix products, body(): jnp.dot(shaped.reshape(block_rows * window_count, sample_count), dft_tabl...  11.4 us
    reshape x1, local copies, waits for them, and re-layouts, body(): ordered.transpose(3, 2, 1, 0)  9.13 us
  transfers between devices with their start and end apart: 1, of which 1 were waited for; matrix products, arithmetic and copies ran while one was open for 1% of the time, Pallas kernels for 0%

profile of v1, /device:TPU:0, one launch (start us, length us, event | category | flops | bytes accessed | tf_op | source)
XLA Modules:
  0.0 211.9 jit_solution(890742625696735108)
XLA Ops:
  6.5 0.2 multiply_subtract_fusion
  6.7 0.9 fusion.16
  7.6 1.1 fusion.9
  8.7 12.4 %subtract_convert_fusion = (bf16[120,100,512]{2,1,0:T(8,128)(2,1)}, bf16[120,100,512]{2,1,0:T(8,128)(2,1)}) fusion(f32[100,512]{1,0:T(8,128)S(1)} %get-tuple-element.16, f32[120,512]{1,0:T(8,128)S(1)} %get-tuple-element.14, f32[100,512]{1,0:T(8,128)S(1)} %get-tuple-element.15, f32[120,512]{1,0:T(8,128)S(1)} %get-tuple-element.13), kind=kLoop, calls=%fused_computation.4 | loop fusion | flops 55296000 | bytes 25477120 | tf_op jit(solution)/shard_map/convert.3
  21.0 16.1 %neg.18 = bf16[12000,512]{1,0:T(8,128)(2,1)} reshape(bf16[120,100,512]{2,1,0:T(8,128)(2,1)} %get-tuple-element.8) | data formatting | bytes 24576000 | tf_op jit(solution)/shard_map/neg | solution.py:29
  37.1 16.1 %sub.26 = bf16[12000,512]{1,0:T(8,128)(2,1)} reshape(bf16[120,100,512]{2,1,0:T(8,128)(2,1)} %get-tuple-element.7) | data formatting | bytes 24576000 | tf_op jit(solution)/shard_map/sub | solution.py:27
  53.2 20.5 %maximum_bitcast_fusion = bf16[1024,12000]{0,1:T(8,128)(2,1)} fusion(bf16[12000,512]{1,0:T(8,128)(2,1)} %neg.18, bf16[12000,512]{1,0:T(8,128)(2,1)} %sub.26), kind=kLoop, calls=%fused_computation.5 | loop fusion | flops 49152000 | bytes 49152000 | tf_op jit(solution)/shard_map/dot_general | solution.py:58
  73.7 32.7 %copy.16 = bf16[1024,12000]{1,0:T(8,128)(2,1)} copy(bf16[1024,12000]{0,1:T(8,128)(2,1)} %maximum_bitcast_fusion) | data formatting | bytes 49152000 | tf_op jit(solution)/shard_map/dot_general | solution.py:58
  106.4 1.3 fusion
  107.7 1.5 fusion.3
  109.2 11.4 %multiply_reduce_fusion = (f32[128,16]{0,1:T(8,128)S(1)}, f32[128,2,16,32]{0,3,2,1:T(8,128)S(1)}) fusion(bf16[128,12000,1,1]{1,0,3,2:T(8,128)(2,1)S(1)} %bitcast.35, bf16[2,16,32,12000]{3,2,1,0:T(8,128)(2,1)} %bitcast.33), kind=kOutput, calls=%fused_computation.17 | convolution fusion | flops 3145988096 | bytes 28180480 | tf_op jit(solution)/shard_map/dot_general | solution.py:58
  120.7 0.8 copy.18
  121.5 1.0 convert_element_type.62
  122.6 0.1 broadcast_multiply_fusion
  122.7 0.7 copy.19
  123.4 1.2 scatter_custom_fusion
  124.7 51.9 %all-gather.2.cloned.1.call-done = bf16[128,16,2,512]{3,1,2,0:T(8,128)(2,1)} async-done(((bf16[8,16,2,512]{3,1,2,0:T(8,128)(2,1)}), bf16[128,16,2,512]{3,1,2,0:T(8,128)(2,1)}) %all-gather.2.cloned.1.call-update) | async-done | bytes 4194320 | tf_op jit(solution)/shard_map/all_gather | solution.py:69
  176.7 2.7 %gather_fusion = bf16[8,16,2,512]{3,1,2,0:T(8,128)(2,1)S(1)} fusion(bf16[128,16,2,512]{3,1,2,0:T(8,128)(2,1)} %all-gather.2.cloned.1.call-done, s32[1024]{0:T(1024)S(1)} %pad_clamp_fusion.1), kind=kCustom, calls=%fused_computation | custom fusion | bytes 524320 | tf_op jit(solution)/shard_map/jit(_take)/gather | solution.py:77
  179.4 0.1 broadcast_select_fusion.1
  179.7 2.0 copy.22
  181.7 4.9 %gather_fusion.1 = bf16[128,16,2,512]{3,1,2,0:T(8,128)(2,1)} fusion(bf16[128,16,2,512]{3,1,2,0:T(8,128)(2,1)} %all-gather.2.cloned.1.call-done, s32[1024]{0:T(1024)S(1)} %pad_clamp_fusion), kind=kCustom, calls=%fused_computation.1 | custom fusion | bytes 8389120 | tf_op jit(solution)/shard_map/jit(_take)/gather | solution.py:75
  186.7 4.6 %broadcast_select_fusion = bf16[128,16,2,512]{3,1,2,0:T(8,128)(2,1)} fusion(bf16[128,16,2,512]{3,1,2,0:T(8,128)(2,1)} %gather_fusion.1, pred[128]{0:T(512)(128)(4,1)S(1)} %compare_and_fusion), kind=kLoop, calls=%fused_computation.14 | loop fusion | flops 2097152 | bytes 8388736 | tf_op jit(solution)/shard_map/jit(_take)/select_n | solution.py:75
  191.2 9.1 %copy.23 = bf16[512,32,128]{2,1,0:T(8,128)(2,1)} copy(bf16[512,32,128]{0,1,2:T(8,128)(2,1)} %bitcast.34) | data formatting | bytes 8388608 | tf_op jit(solution)/shard_map/reshape | solution.py:84
  200.4 4.7 %multiply_convert_fusion = bf16[512,16,128]{2,1,0:T(8,128)(2,1)} fusion(bf16[512,16,32]{2,1,0:T(8,128)(2,1)S(1)} %copy.22, bf16[512,32,128]{2,1,0:T(8,128)(2,1)} %copy.23), kind=kOutput, calls=%fused_computation.13 | convolution fusion | flops 69206016 | bytes 6815744 | tf_op jit(solution)/shard_map/bik,bkj->bij/dot_general | solution.py:85
  (28 shorter events, 0.5 us)
Async XLA Ops:
  6.5 170.1 %all-gather.2.cloned.1.call-start = ((), (), s32[]{:S(2)}) async-start(), calls=%async_computation | async-start | bytes 4456448 | tf_op jit(solution)/shard_map/all_gather | solution.py:69
  73.7 32.7 %copy-start = (bf16[8,16,12000]{2,1,0:T(8,128)(2,1)S(1)}, bf16[8,16,12000]{2,1,0:T(8,128)(2,1)}, u32[]{:S(2)}) copy-start(bf16[8,16,12000]{2,1,0:T(8,128)(2,1)} %param.4) | copy-start | bytes 9216004
  73.7 32.7 %copy-start.1 = (s32[8,16]{1,0:T(8,128)S(1)}, s32[8,16]{1,0:T(8,128)}, u32[]{:S(2)}) copy-start(s32[8,16]{1,0:T(8,128)} %param.5) | copy-start | bytes 1540
  109.2 13.3 %copy-start.2 = (s32[128]{0:T(128)S(1)}, s32[128]{0:T(128)}, u32[]{:S(2)}) copy-start(s32[128]{0:T(128)} %param.6) | copy-start | bytes 1540
  109.2 14.2 %copy-start.3 = (s32[128]{0:T(128)S(1)}, s32[128]{0:T(128)}, u32[]{:S(2)}) copy-start(s32[128]{0:T(128)} %param.7) | copy-start | bytes 1540
Sparse Core Ops, SparseCore 0:
  123.5 53.0 all-gather.1

commit v2 on v1

--- a/solution.py
+++ b/solution.py
@@ -3,37 +3,84 @@
 import jax
 import jax.numpy as jnp
 from jax import lax
+from jax.experimental import pallas as pl
+from jax.experimental.pallas import tpu as pltpu
 from jax.sharding import PartitionSpec as P
 
 WIN = 12000
 NB = 512
 K0 = 6
 SUB = 32
-SPLIT = 100
+LANE = 128
+PADDED = 12288
+TILES_PER_STEP = 8
 
 
 def small_table(sample_values):
     bin_index = K0 + jnp.arange(NB, dtype=jnp.int32)
     residue = sample_values[:, None] * bin_index[None, :] % WIN
     angles = residue.astype(jnp.float32) * (2.0 * math.pi / WIN)
-    return jnp.cos(angles), jnp.sin(angles)
+    return jnp.cos(angles), -jnp.sin(angles)
 
 
-def dft_table():
-    high = jnp.arange(WIN // SPLIT, dtype=jnp.int32) * SPLIT
-    low = jnp.arange(SPLIT, dtype=jnp.int32)
-    cos_high, sin_high = small_table(high)
-    cos_low, sin_low = small_table(low)
-    cos_all = cos_high[:, None, :] * cos_low[None, :, :] - sin_high[:, None, :] * sin_low[None, :, :]
-    sin_all = sin_high[:, None, :] * cos_low[None, :, :] + cos_high[:, None, :] * sin_low[None, :, :]
-    table = jnp.concatenate([cos_all, -sin_all], axis=2).astype(jnp.bfloat16)
-    return table.reshape(WIN, 2 * NB)
+def dft_kernel(x_ref, cos_high_ref, sin_high_ref, cos_low_ref, sin_low_ref, out_ref):
+    step = pl.program_id(0)
+
+    @pl.when(step == 0)
+    def _():
+        out_ref[...] = jnp.zeros_like(out_ref)
+
+    cos_low = cos_low_ref[...]
+    sin_low = sin_low_ref[...]
+    real_total = out_ref[:, :NB]
+    imag_total = out_ref[:, NB:]
+    for tile in range(TILES_PER_STEP):
+        row = step * TILES_PER_STEP + tile
+        cos_high = cos_high_ref[pl.ds(row, 1), :]
+        sin_high = sin_high_ref[pl.ds(row, 1), :]
+        cos_part = (cos_high * cos_low - sin_high * sin_low).astype(jnp.bfloat16)
+        sin_part = (sin_high * cos_low + cos_high * sin_low).astype(jnp.bfloat16)
+        samples = x_ref[:, tile * LANE:(tile + 1) * LANE]
+        real_total = real_total + jnp.dot(samples, cos_part, preferred_element_type=jnp.float32)
+        imag_total = imag_total + jnp.dot(samples, sin_part, preferred_element_type=jnp.float32)
+    out_ref[:, :NB] = real_total
+    out_ref[:, NB:] = imag_total
+
+
+def spectra_of(shaped_rows):
+    row_count = shaped_rows.shape[0]
+    high_count = PADDED // LANE
+    cos_high, sin_high = small_table(jnp.arange(high_count, dtype=jnp.int32) * LANE)
+    cos_low, sin_low = small_table(jnp.arange(LANE, dtype=jnp.int32))
+    block = TILES_PER_STEP * LANE
+    steps = PADDED // block
+    full = lambda shape: pl.BlockSpec(shape, lambda s: (0, 0))
+    return pl.pallas_call(
+        dft_kernel,
+        out_shape=jax.ShapeDtypeStruct((row_count, 2 * NB), jnp.float32),
+        grid=(steps,),
+        in_specs=[
+            pl.BlockSpec((row_count, block), lambda s: (0, s)),
+            full((high_count, NB)),
+            full((high_count, NB)),
+            full((LANE, NB)),
+            full((LANE, NB)),
+        ],
+        out_specs=full((row_count, 2 * NB)),
+        compiler_params=pltpu.CompilerParams(dimension_semantics=("arbitrary",)),
+        cost_estimate=pl.CostEstimate(
+            flops=2 * row_count * PADDED * 2 * NB,
+            transcendentals=0,
+            bytes_accessed=row_count * PADDED * 2 + row_count * 2 * NB * 4,
+        ),
+    )(shaped_rows, cos_high, sin_high, cos_low, sin_low)
 
 
 def prepare(raw_block, valid_lengths):
-    positions = jnp.arange(WIN, dtype=jnp.int32)
+    positions = jnp.arange(PADDED, dtype=jnp.int32)
     inside = positions[None, None, :] < valid_lengths[:, :, None]
-    values = raw_block.astype(jnp.float32)
+    pad = ((0, 0), (0, 0), (0, PADDED - raw_block.shape[2]))
+    values = jnp.pad(raw_block, pad).astype(jnp.float32)
     kept = jnp.where(inside, values, 0.0)
     average = jnp.sum(kept, axis=-1) / valid_lengths.astype(jnp.float32)
     taper = 0.5 - 0.5 * jnp.cos(positions.astype(jnp.float32) * (2.0 * math.pi / WIN))
@@ -55,11 +102,7 @@
     block_rows, window_count, sample_count = raw.shape
     total_channels = assignment.shape[0]
     shaped = prepare(raw, lengths)
-    spectra = jnp.dot(
-        shaped.reshape(block_rows * window_count, sample_count),
-        dft_table(),
-        preferred_element_type=jnp.float32,
-    )
+    spectra = spectra_of(shaped.reshape(block_rows * window_count, PADDED))
     whitened = whiten(spectra).reshape(block_rows, window_count, 2, NB)
     my_quality = lax.dynamic_slice_in_dim(quality, my_index * block_rows, block_rows)
     whitened = whitened * my_quality.astype(jnp.bfloat16)[:, None, None, None]

time: 214 us -> 124 us (0.58)
  local copies, waits for them, and re-layouts: 87.4 us -> 22.4 us
  other arithmetic: 42.8 us -> 18.5 us
  Pallas kernels: 0 us -> 12.3 us
  matrix products: 16.1 us -> 4.74 us
    dot_general x1 -> x0, local copies, waits for them, and re-layouts: 32.7 us -> none  [body(): jnp.dot(shaped.reshape(block_rows * window_count, sample_count), dft_tabl...]
    dot_general x1 -> x0, other arithmetic: 20.5 us -> none  [body(): jnp.dot(shaped.reshape(block_rows * window_count, sample_count), dft_tabl...]
    neg x1 -> x0, local copies, waits for them, and re-layouts: 16.1 us -> none  [dft_table(): table = jnp.concatenate([cos_all, -sin_all], axis=2).astype(jnp.bfloat16)]
    sub x1 -> x0, local copies, waits for them, and re-layouts: 16.1 us -> none  [dft_table(): cos_high[:, None, :] * cos_low[None, :, :]]
    another operation x1 -> x0, other arithmetic: 12.4 us -> none
    pallas_call x0 -> x1, Pallas kernels: none -> 12.3 us  [spectra_of(): pl.pallas_call(dft_kernel, out_shape=jax.ShapeDtypeStruct((row_count, 2 *...]
    dot_general x1 -> x0, matrix products: 11.4 us -> none  [body(): jnp.dot(shaped.reshape(block_rows * window_count, sample_count), dft_tabl...]
    neg x0 -> x2, other arithmetic: none -> 3.45 us  [small_table(): return (jnp.cos(angles), -jnp.sin(angles))]
where the time goes in v2:
time: 124 us
  waiting for transfers between devices  52.1 us (42%)
  local copies, waits for them, and re-layouts  22.4 us (18%)
  other arithmetic  18.5 us (15%)
  between operations  13.5 us (11%)
  Pallas kernels  12.3 us (10%)
  matrix products  4.74 us (4%)
    all_gather x1, waiting for transfers between devices, body(): gathered = lax.all_gather(panel, 'chan', axis=0, tiled=True)  52.1 us
    pallas_call x1, Pallas kernels, spectra_of(): pl.pallas_call(dft_kernel, out_shape=jax.ShapeDtypeStruct((row_count, 2 *...  12.3 us
    reshape x1, local copies, waits for them, and re-layouts, body(): ordered.transpose(3, 2, 1, 0)  9.12 us
    gather x1, local copies, waits for them, and re-layouts, body(): ordered = jnp.take(gathered, inverse, axis=0)  4.97 us
    dot_general x1, matrix products, body(): jnp.einsum('bik,bkj->bij', left_rows, right, preferred_element_type=jnp.f...  4.74 us
    select_n x2, other arithmetic, body(): ordered = jnp.take(gathered, inverse, axis=0)  4.61 us
    convert_element_type x1, other arithmetic, prepare(): jnp.where(inside, (values - average[:, :, None]) * taper[None, None, :],...  3.83 us
    neg x2, other arithmetic, small_table(): return (jnp.cos(angles), -jnp.sin(angles))  3.45 us
  transfers between devices with their start and end apart: 1, of which 1 were waited for; matrix products, arithmetic and copies ran while one was open for 1% of the time, Pallas kernels for 0%

profile of v2, /device:TPU:0, one launch (start us, length us, event | category | flops | bytes accessed | tf_op | source)
XLA Modules:
  0.0 123.6 jit_solution(9121980203274945737)
XLA Ops:
  6.5 0.2 multiply_subtract_fusion
  6.7 3.2 %fusion = f32[8,16]{1,0:T(8,128)S(1)} fusion(s32[8,16]{1,0:T(8,128)} %param.5, bf16[8,16,12000]{2,1,0:T(8,128)(2,1)} %param.4), kind=kLoop, calls=%fused_computation.5 | loop fusion | flops 6291328 | bytes 3073024 | tf_op jit(solution)/shard_map/reduce_sum | solution.py:85
  9.9 0.7 convert_divide_fusion
  10.6 1.8 %sine_negate_fusion = (f32[128,512]{1,0:T(8,128)}, f32[128,512]{1,0:T(8,128)}) fusion(s32[512]{0:T(512)S(1)} %iota_add_fusion), kind=kLoop, calls=%fused_computation.22 | loop fusion | flops 655360 | bytes 526336 | tf_op jit(solution)/shard_map/neg | solution.py:23
  12.5 1.6 %sine_negate_fusion.1 = (f32[96,512]{1,0:T(8,128)}, f32[96,512]{1,0:T(8,128)}) fusion(s32[512]{0:T(512)S(1)} %iota_add_fusion, s32[96]{0:T(128)S(1)} %iota_multiply_fusion), kind=kLoop, calls=%fused_computation.31 | loop fusion | flops 491520 | bytes 395648 | tf_op jit(solution)/shard_map/neg | solution.py:23
  14.1 3.8 %fusion.3 = bf16[8,16,12288]{2,1,0:T(8,128)(2,1)} fusion(f32[12288]{0:T(1024)S(1)} %multiply_subtract_fusion, f32[8,16]{1,0:T(8,128)S(1)} %convert_divide_fusion, s32[8,16]{1,0:T(8,128)} %param.5, bf16[8,16,12000]{2,1,0:T(8,128)(2,1)S(1)} %copy-done), kind=kLoop, calls=%fused_computation.8 | loop fusion | flops 9437184 | bytes 6267904 | tf_op jit(solution)/shard_map/convert_element_type | solution.py:87
  17.9 12.3 %shard_map.46 = f32[128,1024]{1,0:T(8,128)} custom-call(bf16[128,12288]{1,0:T(8,128)(2,1)} %bitcast.23, f32[96,512]{1,0:T(8,128)} %get-tuple-element.12.cos_high_ref, f32[96,512]{1,0:T(8,128)} %get-tuple-element.11.sin_high_ref, f32[128,512]{1,0:T(8,128)} %get-tuple-element.14.cos_low_ref, f32[128,512]{1,0:T(8,128)} %get-tuple-element.13.sin_low_ref), custom_call_target="tpu_custom_call" | custom-call | flops 3221225472 | bytes 3670016 | tf_op jit(solution)/shard_map/pallas_call | solution.py:58
  30.2 1.3 %mul.141 = f32[128,1024]{1,0:T(8,128)S(1)} multiply(f32[128,1024]{1,0:T(8,128)} %shard_map.46, f32[128,1024]{1,0:T(8,128)} %shard_map.46) | non-fusion elementwise | flops 131072 | bytes 1572864 | tf_op jit(solution)/shard_map/mul | solution.py:95
  31.5 1.5 %reshape.68 = f32[8,16,2,512]{3,2,1,0:T(2,128)S(1)} reshape(f32[128,1024]{1,0:T(8,128)} %shard_map.46) | data formatting | bytes 1048576 | tf_op jit(solution)/shard_map/reshape | solution.py:94
  33.0 0.2 copy.17
  33.2 0.1 copy.18
  33.3 0.3 mul.143
  33.7 0.4 mul.144
  34.2 0.8 fusion.7
  35.1 1.0 scatter_custom_fusion
  36.0 0.1 compare_and_fusion.1
  36.2 52.1 %all-gather.2.cloned.1.call-done = bf16[128,16,2,512]{3,1,2,0:T(8,128)(2,1)} async-done(((bf16[8,16,2,512]{3,1,2,0:T(8,128)(2,1)}), bf16[128,16,2,512]{3,1,2,0:T(8,128)(2,1)}) %all-gather.2.cloned.1.call-update) | async-done | bytes 4194320 | tf_op jit(solution)/shard_map/all_gather | solution.py:112
  88.3 2.7 %gather_fusion = bf16[8,16,2,512]{3,1,2,0:T(8,128)(2,1)S(1)} fusion(bf16[128,16,2,512]{3,1,2,0:T(8,128)(2,1)} %all-gather.2.cloned.1.call-done, s32[1024]{0:T(1024)S(1)} %pad_clamp_fusion.1), kind=kCustom, calls=%fused_computation | custom fusion | bytes 524320 | tf_op jit(solution)/shard_map/jit(_take)/gather | solution.py:120
  91.0 0.1 broadcast_select_fusion.1
  91.2 5.0 %gather_fusion.1 = bf16[128,16,2,512]{3,1,2,0:T(8,128)(2,1)} fusion(bf16[128,16,2,512]{3,1,2,0:T(8,128)(2,1)} %all-gather.2.cloned.1.call-done, s32[1024]{0:T(1024)S(1)} %pad_clamp_fusion), kind=kCustom, calls=%fused_computation.1 | custom fusion | bytes 8389120 | tf_op jit(solution)/shard_map/jit(_take)/gather | solution.py:118
  96.1 4.6 %broadcast_select_fusion = bf16[128,16,2,512]{3,1,2,0:T(8,128)(2,1)} fusion(bf16[128,16,2,512]{3,1,2,0:T(8,128)(2,1)} %gather_fusion.1, pred[128]{0:T(512)(128)(4,1)S(1)} %compare_and_fusion), kind=kLoop, calls=%fused_computation.11 | loop fusion | flops 2097152 | bytes 8388736 | tf_op jit(solution)/shard_map/jit(_take)/select_n | solution.py:118
  100.7 9.1 %copy.22 = bf16[512,32,128]{2,1,0:T(8,128)(2,1)} copy(bf16[512,32,128]{0,1,2:T(8,128)(2,1)} %bitcast.22) | data formatting | bytes 8388608 | tf_op jit(solution)/shard_map/reshape | solution.py:127
  110.0 2.0 %copy.21 = bf16[512,16,32]{2,1,0:T(8,128)(2,1)S(1)} copy(bf16[512,16,32]{0,2,1:T(8,128)(2,1)S(1)} %bitcast.24) | data formatting | bytes 1048576 | tf_op jit(solution)/shard_map/reshape | solution.py:126
  112.0 4.7 %multiply_convert_fusion = bf16[512,16,128]{2,1,0:T(8,128)(2,1)} fusion(bf16[512,16,32]{2,1,0:T(8,128)(2,1)S(1)} %copy.21, bf16[512,32,128]{2,1,0:T(8,128)(2,1)} %copy.22), kind=kOutput, calls=%fused_computation.10 | convolution fusion | flops 69206016 | bytes 6815744 | tf_op jit(solution)/shard_map/bik,bkj->bij/dot_general | solution.py:128
  (24 shorter events, 0.4 us)
Async XLA Ops:
  6.5 7.6 %copy-start = (bf16[8,16,12000]{2,1,0:T(8,128)(2,1)S(1)}, bf16[8,16,12000]{2,1,0:T(8,128)(2,1)}, u32[]{:S(2)}) copy-start(bf16[8,16,12000]{2,1,0:T(8,128)(2,1)} %param.4) | copy-start | bytes 9216004
  6.5 81.7 %all-gather.2.cloned.1.call-start = ((), (), s32[]{:S(2)}) async-start(), calls=%async_computation | async-start | bytes 4456448 | tf_op jit(solution)/shard_map/all_gather | solution.py:112
  30.2 3.9 %copy-start.1 = (s32[128]{0:T(128)S(1)}, s32[128]{0:T(128)}, u32[]{:S(2)}) copy-start(s32[128]{0:T(128)} %param.6) | copy-start | bytes 1540
  30.2 4.8 %copy-start.2 = (s32[128]{0:T(128)S(1)}, s32[128]{0:T(128)}, u32[]{:S(2)}) copy-start(s32[128]{0:T(128)} %param.7) | copy-start | bytes 1540
Sparse Core Ops, SparseCore 0:
  35.1 53.0 all-gather.1

commit v3 on v1

v3 whole, which is shorter than its diff:
```python
import math

import numpy as np

import jax
import jax.numpy as jnp
from jax import lax
from jax.experimental import pallas as pl
from jax.experimental.pallas import tpu as pltpu
from jax.sharding import PartitionSpec as P

WIN = 12000
NB = 512
K0 = 6
SUB = 32
LANE = 128
PADDED = 12288
TILES_PER_STEP = 8


def small_table(sample_values):
    bin_index = K0 + np.arange(NB, dtype=np.int64)
    residue = sample_values[:, None] * bin_index[None, :] % WIN
    angles = residue.astype(np.float64) * (2.0 * math.pi / WIN)
    return np.cos(angles).astype(np.float32), (-np.sin(angles)).astype(np.float32)


def constant_tables():
    high_count = PADDED // LANE
    cos_high, sin_high = small_table(np.arange(high_count, dtype=np.int64) * LANE)
    cos_low, sin_low = small_table(np.arange(LANE, dtype=np.int64))
    positions = np.arange(PADDED, dtype=np.float64)
    taper = (0.5 - 0.5 * np.cos(positions * (2.0 * math.pi / WIN))).astype(np.float32)
    groups = (np.arange(NB)[:, None] // SUB == np.arange(NB // SUB)[None, :]).astype(np.float32)
    return cos_high, sin_high, cos_low, sin_low, taper.reshape(1, PADDED), groups


def dft_kernel(
    raw_ref, length_ref, quality_ref, taper_ref, cos_high_ref, sin_high_ref, cos_low_ref,
    sin_low_ref, groups_ref, out_ref, total_ref, mean_ref,
):
    phase = pl.program_id(0)
    step = pl.program_id(1)
    block = TILES_PER_STEP * LANE
    lengths = length_ref[...]

    @pl.when(jnp.logical_and(phase == 0, step == 0))
    def _():
        mean_ref[...] = jnp.zeros_like(mean_ref)
        total_ref[...] = jnp.zeros_like(total_ref)

    @pl.when(phase == 0)
    def _():
        positions = step * block + lax.broadcasted_iota(jnp.int32, raw_ref.shape, 1)
        inside = positions < lengths
        kept = jnp.where(inside, raw_ref[...].astype(jnp.float32), 0.0)
        mean_ref[...] += jnp.sum(kept, axis=1, keepdims=True)

    @pl.when(phase == 1)
    def _():
        average = mean_ref[...] / lengths.astype(jnp.float32)
        cos_low = cos_low_ref[...]
        sin_low = sin_low_ref[...]
        real_total = total_ref[:, :NB]
        imag_total = total_ref[:, NB:]
        for tile in range(TILES_PER_STEP):
            row = step * TILES_PER_STEP + tile
            cos_high = cos_high_ref[pl.ds(row, 1), :]
            sin_high = sin_high_ref[pl.ds(row, 1), :]
            cos_part = (cos_high * cos_low - sin_high * sin_low).astype(jnp.bfloat16)
            sin_part = (sin_high * cos_low + cos_high * sin_low).astype(jnp.bfloat16)
            values = raw_ref[:, tile * LANE:(tile + 1) * LANE].astype(jnp.float32)
            positions = row * LANE + lax.broadcasted_iota(jnp.int32, values.shape, 1)
            taper = taper_ref[:, pl.ds(pl.multiple_of(row * LANE, LANE), LANE)]
            samples = jnp.where(
                positions < lengths, (values - average) * taper, 0.0
            ).astype(jnp.bfloat16)
            real_total = real_total + jnp.dot(samples, cos_part, preferred_element_type=jnp.float32)
            imag_total = imag_total + jnp.dot(samples, sin_part, preferred_element_type=jnp.float32)
        total_ref[:, :NB] = real_total
        total_ref[:, NB:] = imag_total

        @pl.when(step == pl.num_programs(1) - 1)
        def _():
            groups = groups_ref[...]
            power = jnp.dot(
                real_total * real_total + imag_total * imag_total,
                groups,
                precision=lax.Precision.HIGHEST,
                preferred_element_type=jnp.float32,
            ) / SUB
            factor = lax.rsqrt(power + 1e-06)
            spread = lax.dot_general(
                factor, groups, (((1,), (1,)), ((), ())),
                precision=lax.Precision.HIGHEST,
                preferred_element_type=jnp.float32,
            )
            good = quality_ref[...] != 0
            real_out = (real_total * spread).astype(jnp.bfloat16)
            imag_out = (imag_total * spread).astype(jnp.bfloat16)
            zero = jnp.zeros_like(real_out)
            out_ref[:, :NB] = jnp.where(good, real_out, zero)
            out_ref[:, NB:] = jnp.where(good, imag_out, zero)


def whitened_of(raw_rows, length_rows, quality_rows):
    row_count = raw_rows.shape[0]
    tables = [jnp.asarray(t) for t in constant_tables()]
    block = TILES_PER_STEP * LANE
    steps = PADDED // block
    full = lambda shape: pl.BlockSpec(shape, lambda p, s: (0, 0))
    return pl.pallas_call(
        dft_kernel,
        out_shape=jax.ShapeDtypeStruct((row_count, 2 * NB), jnp.bfloat16),
        grid=(2, steps),
        in_specs=[
            pl.BlockSpec((row_count, block), lambda p, s: (0, s)),
            full((row_count, 1)),
            full((row_count, 1)),
            full((1, PADDED)),
            full(tables[1].shape),
            full(tables[1].shape),
            full(tables[2].shape),
            full(tables[2].shape),
            full(tables[5].shape),
        ],
        out_specs=full((row_count, 2 * NB)),
        scratch_shapes=[
            pltpu.VMEM((row_count, 2 * NB), jnp.float32),
            pltpu.VMEM((row_count, 1), jnp.float32),
        ],
        compiler_params=pltpu.CompilerParams(dimension_semantics=("arbitrary", "arbitrary")),
        cost_estimate=pl.CostEstimate(
            flops=2 * row_count * PADDED * 2 * NB,
            transcendentals=0,
            bytes_accessed=2 * row_count * WIN * 2 + row_count * 2 * NB * 2,
        ),
    )(raw_rows, length_rows, quality_rows, tables[4], tables[0], tables[1], tables[2], tables[3], tables[5])


def body(raw, lengths, quality, assignment):
    my_index = lax.axis_index("chan")
    block_rows, window_count, sample_count = raw.shape
    total_channels = assignment.shape[0]
    row_count = block_rows * window_count
    my_quality = lax.dynamic_slice_in_dim(quality, my_index * block_rows, block_rows)
    quality_rows = jnp.broadcast_to(my_quality[:, None], (block_rows, window_count))
    whitened = whitened_of(
        raw.reshape(row_count, sample_count),
        lengths.reshape(row_count, 1),
        quality_rows.reshape(row_count, 1),
    ).reshape(block_rows, window_count, 2, NB)
    panel = lax.all_to_all(whitened, "freq", split_axis=3, concat_axis=1, tiled=True)
    all_windows = panel.shape[1]
    bins_here = panel.shape[3]
    gathered = lax.all_gather(panel, "chan", axis=0, tiled=True)
    inverse = (
        jnp.zeros((total_channels,), jnp.int32)
        .at[assignment]
        .set(jnp.arange(total_channels, dtype=jnp.int32))
    )
    ordered = jnp.take(gathered, inverse, axis=0)
    mine = lax.dynamic_slice_in_dim(inverse, my_index * block_rows, block_rows)
    left = jnp.take(gathered, mine, axis=0)
    left_re = left[:, :, 0, :]
    left_im = left[:, :, 1, :]
    plain = jnp.stack([left_re, left_im], axis=1)
    turned = jnp.stack([left_im, -left_re], axis=1)
    left_rows = jnp.stack([plain, turned], axis=1)
    left_rows = left_rows.transpose(4, 0, 1, 2, 3).reshape(bins_here, block_rows * 2, 2 * all_windows)
    right = ordered.transpose(3, 2, 1, 0).reshape(bins_here, 2 * all_windows, total_channels)
    out = jnp.einsum("bik,bkj->bij", left_rows, right, preferred_element_type=jnp.float32)
    return (out / all_windows).astype(jnp.bfloat16).reshape(bins_here, block_rows, 2, total_channels)


def solution(mesh):
    return jax.shard_map(
        body,
        mesh=mesh,
        in_specs=(
            P(("groups", "chan"), "freq", None),
            P(("groups", "chan"), "freq"),
            P("groups"),
            P("groups"),
        ),
        out_specs=P("freq", ("groups", "chan"), None, None),
        check_vma=False,
    )
```

time: 214 us -> 122 us (0.57)
  local copies, waits for them, and re-layouts: 87.4 us -> 24.7 us
  other arithmetic: 42.8 us -> 4.92 us
  Pallas kernels: 0 us -> 21 us
  matrix products: 16.1 us -> 4.74 us
    dot_general x1 -> x0, local copies, waits for them, and re-layouts: 32.7 us -> none  [body(): jnp.dot(shaped.reshape(block_rows * window_count, sample_count), dft_tabl...]
    pallas_call x0 -> x1, Pallas kernels: none -> 21 us  [whitened_of(): pl.pallas_call(dft_kernel, out_shape=jax.ShapeDtypeStruct((row_count, 2 *...]
    dot_general x1 -> x0, other arithmetic: 20.5 us -> none  [body(): jnp.dot(shaped.reshape(block_rows * window_count, sample_count), dft_tabl...]
    neg x1 -> x0, local copies, waits for them, and re-layouts: 16.1 us -> none  [dft_table(): table = jnp.concatenate([cos_all, -sin_all], axis=2).astype(jnp.bfloat16)]
    sub x1 -> x0, local copies, waits for them, and re-layouts: 16.1 us -> none  [dft_table(): cos_high[:, None, :] * cos_low[None, :, :]]
    another operation x1 -> x0, other arithmetic: 12.4 us -> none
    dot_general x1 -> x0, matrix products: 11.4 us -> none  [body(): jnp.dot(shaped.reshape(block_rows * window_count, sample_count), dft_tabl...]
    reshape x0 -> x4, local copies, waits for them, and re-layouts: none -> 3.98 us  [the longest x2 1.89 us: body(): whitened = whitened_of(raw.reshape(row_count, sample_count), lengths.resh...]
where the time goes in v3:
time: 122 us; the launch traced here: 121 us
  waiting for transfers between devices  52.1 us (43%)
  local copies, waits for them, and re-layouts  24.7 us (20%)
  Pallas kernels  21 us (17%)
  between operations  13.5 us (11%)
  other arithmetic  4.92 us (4%)
  matrix products  4.74 us (4%)
    all_gather x1, waiting for transfers between devices, body(): gathered = lax.all_gather(panel, 'chan', axis=0, tiled=True)  52.1 us
    pallas_call x1, Pallas kernels, whitened_of(): pl.pallas_call(dft_kernel, out_shape=jax.ShapeDtypeStruct((row_count, 2 *...  21 us
    reshape x1, local copies, waits for them, and re-layouts, body(): ordered.transpose(3, 2, 1, 0)  9.12 us
    gather x1, local copies, waits for them, and re-layouts, body(): ordered = jnp.take(gathered, inverse, axis=0)  4.98 us
    dot_general x1, matrix products, body(): jnp.einsum('bik,bkj->bij', left_rows, right, preferred_element_type=jnp.f...  4.74 us
    select_n x2, other arithmetic, body(): ordered = jnp.take(gathered, inverse, axis=0)  4.62 us
    gather x1, local copies, waits for them, and re-layouts, body(): left = jnp.take(gathered, mine, axis=0)  2.75 us
  transfers between devices with their start and end apart: 1, of which 1 were waited for; matrix products, arithmetic and copies ran while one was open for 1% of the time, Pallas kernels for 0%

profile of v3, /device:TPU:0, one launch (start us, length us, event | category | flops | bytes accessed | tf_op | source)
XLA Modules:
  0.0 121.0 jit_solution(17141213844049730746)
XLA Ops:
  6.5 0.0 all-gather.2.cloned.1.call-start
  6.5 0.7 dynamic_slice.7
  7.3 0.1 broadcast_in_dim.35
  7.3 0.7 reshape.77.quality_ref
  8.0 1.4 %reshape.76.length_ref = s32[128,1]{1,0:T(8,128)} reshape(s32[8,16]{1,0:T(8,128)} %param.11) | data formatting | bytes 1024 | tf_op jit(solution)/shard_map/reshape | solution.py:150
  9.4 0.0 copy-start
  9.4 21.0 %shard_map.100 = bf16[128,1024]{1,0:T(8,128)(2,1)} custom-call(bf16[128,12000]{1,0:T(8,128)(2,1)} %bitcast.23, s32[128,1]{1,0:T(8,128)} %reshape.76.length_ref, s32[128,1]{1,0:T(8,128)} %reshape.77.quality_ref, f32[1,12288]{1,0:T(1,128)} %constant.57.clone.taper_ref, f32[96,512]{1,0:T(8,128)} %constant.53.clone.cos_high_ref, ...), custom_call_target="tpu_custom_call" | custom-call | flops 3221225472 | bytes 6406144 | tf_op jit(solution)/shard_map/pallas_call | solution.py:112
  30.5 1.1 reshape.45
  31.6 0.7 copy.29
  32.4 0.0 all-gather.2.cloned.1.call-update
  32.4 0.0 copy-done
  32.4 1.0 scatter_custom_fusion
  33.4 0.1 compare_and_fusion.1
  33.5 52.1 %all-gather.2.cloned.1.call-done = bf16[128,16,2,512]{3,1,2,0:T(8,128)(2,1)} async-done(((bf16[8,16,2,512]{3,1,2,0:T(8,128)(2,1)}), bf16[128,16,2,512]{3,1,2,0:T(8,128)(2,1)}) %all-gather.2.cloned.1.call-update) | async-done | bytes 4194320 | tf_op jit(solution)/shard_map/all_gather | solution.py:156
  85.6 2.7 %gather_fusion = bf16[8,16,2,512]{3,1,2,0:T(8,128)(2,1)S(1)} fusion(bf16[128,16,2,512]{3,1,2,0:T(8,128)(2,1)} %all-gather.2.cloned.1.call-done, s32[1024]{0:T(1024)S(1)} %pad_clamp_fusion.1), kind=kCustom, calls=%fused_computation | custom fusion | bytes 524320 | tf_op jit(solution)/shard_map/jit(_take)/gather | solution.py:164
  88.4 0.1 broadcast_select_fusion.1
  88.5 5.0 %gather_fusion.1 = bf16[128,16,2,512]{3,1,2,0:T(8,128)(2,1)} fusion(bf16[128,16,2,512]{3,1,2,0:T(8,128)(2,1)} %all-gather.2.cloned.1.call-done, s32[1024]{0:T(1024)S(1)} %pad_clamp_fusion), kind=kCustom, calls=%fused_computation.1 | custom fusion | bytes 8389120 | tf_op jit(solution)/shard_map/jit(_take)/gather | solution.py:162
  93.5 4.6 %broadcast_select_fusion = bf16[128,16,2,512]{3,1,2,0:T(8,128)(2,1)} fusion(bf16[128,16,2,512]{3,1,2,0:T(8,128)(2,1)} %gather_fusion.1, pred[128]{0:T(512)(128)(4,1)S(1)} %compare_and_fusion), kind=kLoop, calls=%fused_computation.4 | loop fusion | flops 2097152 | bytes 8388736 | tf_op jit(solution)/shard_map/jit(_take)/select_n | solution.py:162
  98.1 9.1 %copy.32 = bf16[512,32,128]{2,1,0:T(8,128)(2,1)} copy(bf16[512,32,128]{0,1,2:T(8,128)(2,1)} %bitcast.21) | data formatting | bytes 8388608 | tf_op jit(solution)/shard_map/reshape | solution.py:171
  107.3 0.1 maximum_bitcast_fusion
  107.4 2.0 %copy.31 = bf16[512,16,32]{2,1,0:T(8,128)(2,1)S(1)} copy(bf16[512,16,32]{0,2,1:T(8,128)(2,1)S(1)} %bitcast.22) | data formatting | bytes 1048576 | tf_op jit(solution)/shard_map/reshape | solution.py:170
  109.4 4.7 %multiply_convert_fusion = bf16[512,16,128]{2,1,0:T(8,128)(2,1)} fusion(bf16[512,16,32]{2,1,0:T(8,128)(2,1)S(1)} %copy.31, bf16[512,32,128]{2,1,0:T(8,128)(2,1)} %copy.32), kind=kOutput, calls=%fused_computation.3 | convolution fusion | flops 69206016 | bytes 6815744 | tf_op jit(solution)/shard_map/bik,bkj->bij/dot_general | solution.py:172
  (10 shorter events, 0.1 us)
Async XLA Ops:
  6.5 79.1 %all-gather.2.cloned.1.call-start = ((), (), s32[]{:S(2)}) async-start(), calls=%async_computation | async-start | bytes 4456448 | tf_op jit(solution)/shard_map/all_gather | solution.py:156
  9.4 23.0 %copy-start = (s32[128]{0:T(128)S(1)}, s32[128]{0:T(128)}, u32[]{:S(2)}) copy-start(s32[128]{0:T(128)} %param.13) | copy-start | bytes 1540
Sparse Core Ops, SparseCore 0:
  32.5 53.0 all-gather.1

commit v4 on v3

--- a/solution.py
+++ b/solution.py
@@ -154,21 +154,20 @@
     all_windows = panel.shape[1]
     bins_here = panel.shape[3]
     gathered = lax.all_gather(panel, "chan", axis=0, tiled=True)
-    inverse = (
-        jnp.zeros((total_channels,), jnp.int32)
-        .at[assignment]
-        .set(jnp.arange(total_channels, dtype=jnp.int32))
+    positions = jnp.arange(total_channels, dtype=jnp.int32)
+    onehot = (assignment[:, None] == positions[None, :]).astype(jnp.bfloat16)
+    right = jnp.einsum(
+        "cwpb,cj->bpwj", gathered, onehot, preferred_element_type=jnp.float32
+    ).astype(jnp.bfloat16).reshape(bins_here, 2 * all_windows, total_channels)
+    mine = my_index * block_rows + jnp.arange(block_rows, dtype=jnp.int32)
+    select = (assignment[:, None] == mine[None, :]).astype(jnp.bfloat16)
+    rotation = jnp.array(
+        [[[1.0, 0.0], [0.0, -1.0]], [[0.0, 1.0], [1.0, 0.0]]], dtype=jnp.bfloat16
     )
-    ordered = jnp.take(gathered, inverse, axis=0)
-    mine = lax.dynamic_slice_in_dim(inverse, my_index * block_rows, block_rows)
-    left = jnp.take(gathered, mine, axis=0)
-    left_re = left[:, :, 0, :]
-    left_im = left[:, :, 1, :]
-    plain = jnp.stack([left_re, left_im], axis=1)
-    turned = jnp.stack([left_im, -left_re], axis=1)
-    left_rows = jnp.stack([plain, turned], axis=1)
-    left_rows = left_rows.transpose(4, 0, 1, 2, 3).reshape(bins_here, block_rows * 2, 2 * all_windows)
-    right = ordered.transpose(3, 2, 1, 0).reshape(bins_here, 2 * all_windows, total_channels)
+    spread = select[:, None, :, None, None] * rotation[None, :, None, :, :]
+    left_rows = jnp.einsum(
+        "cwpb,cpiqr->biqrw", gathered, spread, preferred_element_type=jnp.float32
+    ).astype(jnp.bfloat16).reshape(bins_here, block_rows * 2, 2 * all_windows)
     out = jnp.einsum("bik,bkj->bij", left_rows, right, preferred_element_type=jnp.float32)
     return (out / all_windows).astype(jnp.bfloat16).reshape(bins_here, block_rows, 2, total_channels)
 

time: 122 us -> 119 us (0.975)
  local copies, waits for them, and re-layouts: 24.7 us -> 15.1 us
  matrix products: 4.74 us -> 13.1 us
  other arithmetic: 4.92 us -> 0.08 us
  waiting for transfers between devices: 52.1 us -> 55.3 us
    reshape x2 -> x1, local copies, waits for them, and re-layouts: 11.1 us -> 1.98 us  [body(): left_rows = jnp.einsum('cwpb,cpiqr->biqrw', gathered, spread, preferred_e...]
    dot_general x0 -> x2, matrix products: none -> 8.38 us  [the longest x1 5.37 us: body(): jnp.einsum('cwpb,cj->bpwj', gathered, onehot, preferred_element_type=jnp....]
    convert_element_type x0 -> x2, local copies, waits for them, and re-layouts: none -> 8.22 us  [the longest x1 8.05 us: body(): right = jnp.einsum('cwpb,cj->bpwj', gathered, onehot, preferred_element_t...]
    gather x2 -> x0, local copies, waits for them, and re-layouts: 7.73 us -> none  [the longest x1 4.98 us: body(): ordered = jnp.take(gathered, inverse, axis=0)]
    select_n x4 -> x0, other arithmetic: 4.71 us -> none  [the longest x2 4.62 us: body(): ordered = jnp.take(gathered, inverse, axis=0)]
    all_gather x1, waiting for transfers between devices: 52.1 us -> 55.3 us  [body(): gathered = lax.all_gather(panel, 'chan', axis=0, tiled=True)]
  transfers between devices with their start and end apart: 1 -> 1, of which waited for: 1 -> 1; matrix products, arithmetic and copies ran while one was open for 1% -> 0% of each run, Pallas kernels for 0% -> 0%
where the time goes in v4:
time: 119 us; the launch traced here: 118 us
  waiting for transfers between devices  55.3 us (46%)
  Pallas kernels  21 us (18%)
  local copies, waits for them, and re-layouts  15.1 us (13%)
  between operations  13.4 us (11%)
  matrix products  13.1 us (11%)
    all_gather x1, waiting for transfers between devices, body(): gathered = lax.all_gather(panel, 'chan', axis=0, tiled=True)  55.3 us
    pallas_call x1, Pallas kernels, whitened_of(): pl.pallas_call(dft_kernel, out_shape=jax.ShapeDtypeStruct((row_count, 2 *...  21 us
    convert_element_type x1, local copies, waits for them, and re-layouts, body(): right = jnp.einsum('cwpb,cj->bpwj', gathered, onehot, preferred_element_t...  8.05 us
    dot_general x1, matrix products, body(): jnp.einsum('cwpb,cj->bpwj', gathered, onehot, preferred_element_type=jnp....  5.37 us
    dot_general x1, matrix products, body(): jnp.einsum('bik,bkj->bij', left_rows, right, preferred_element_type=jnp.f...  4.75 us
    dot_general x1, matrix products, body(): jnp.einsum('cwpb,cpiqr->biqrw', gathered, spread, preferred_element_type=...  3.02 us
  transfers between devices with their start and end apart: 1, of which 1 were waited for; matrix products, arithmetic and copies ran while one was open for 0% of the time, Pallas kernels for 0%

profile of v4, /device:TPU:0, one launch (start us, length us, event | category | flops | bytes accessed | tf_op | source)
XLA Modules:
  0.0 118.1 jit_solution(17367317856554069258)
XLA Ops:
  6.5 0.0 all-gather.2.cloned.1.call-start
  6.5 0.7 dynamic_slice.3
  7.3 0.1 broadcast_in_dim.2
  7.3 0.7 reshape.66.quality_ref
  8.1 1.4 %reshape.65.length_ref = s32[128,1]{1,0:T(8,128)} reshape(s32[8,16]{1,0:T(8,128)} %param.12) | data formatting | bytes 1024 | tf_op jit(solution)/shard_map/reshape | solution.py:150
  9.4 0.0 copy-start
  9.4 21.0 %shard_map.109 = bf16[128,1024]{1,0:T(8,128)(2,1)} custom-call(bf16[128,12000]{1,0:T(8,128)(2,1)} %bitcast.41, s32[128,1]{1,0:T(8,128)} %reshape.65.length_ref, s32[128,1]{1,0:T(8,128)} %reshape.66.quality_ref, f32[1,12288]{1,0:T(1,128)} %constant.31.clone.taper_ref, f32[96,512]{1,0:T(8,128)} %constant.27.clone.cos_high_ref, ...), custom_call_target="tpu_custom_call" | custom-call | flops 3221225472 | bytes 6406144 | tf_op jit(solution)/shard_map/pallas_call | solution.py:112
  30.5 1.1 reshape.57
  31.6 0.9 copy.17
  32.5 0.0 all-gather.2.cloned.1.call-update
  32.5 0.0 copy-done
  32.5 0.1 compare_convert_fusion
  32.6 55.3 %all-gather.2.cloned.1.call-done = bf16[128,16,2,512]{3,0,2,1:T(8,128)(2,1)} async-done(((bf16[8,16,2,512]{3,0,2,1:T(8,128)(2,1)}), bf16[128,16,2,512]{3,0,2,1:T(8,128)(2,1)}) %all-gather.2.cloned.1.call-update) | async-done | bytes 4194320 | tf_op jit(solution)/shard_map/all_gather | solution.py:156
  87.9 5.4 %convert_bitcast_fusion = bf16[512,2,16,128]{0,3,1,2:T(8,128)(2,1)} fusion(bf16[128,16,2,512]{3,0,2,1:T(8,128)(2,1)} %all-gather.2.cloned.1.call-done, s32[128]{0:T(128)S(1)} %copy-done), kind=kOutput, calls=%fused_computation.3 | convolution fusion | flops 538984448 | bytes 8389120 | tf_op jit(solution)/shard_map/cwpb,cj->bpwj/dot_general | solution.py:159
  93.3 0.0 copy-start.1
  93.3 8.0 %copy.19 = bf16[512,2,16,128]{3,2,1,0:T(8,128)(2,1)} copy(bf16[512,2,16,128]{0,3,1,2:T(8,128)(2,1)} %convert_bitcast_fusion) | data formatting | bytes 8388608 | tf_op jit(solution)/shard_map/convert_element_type | solution.py:161
  101.3 0.0 copy-done.1
  101.3 3.0 %fusion.8 = bf16[512,8,2,2,16]{0,1,4,3,2:T(8,128)(2,1)S(1)} fusion(bf16[128,16,2,512]{3,0,2,1:T(8,128)(2,1)} %all-gather.2.cloned.1.call-done, bf16[2,2,2]{0,2,1:T(2,128)(2,1)S(1)} %copy-done.1, bf16[128,8]{0,1:T(8,128)(2,1)S(1)} %compare_convert_fusion), kind=kOutput, calls=%fused_computation.6 | convolution fusion | flops 134512640 | bytes 4720656 | tf_op jit(solution)/shard_map/cwpb,cpiqr->biqrw/dot_general | solution.py:168
  104.3 0.2 copy.18
  104.5 2.0 %copy.20 = bf16[512,16,32]{2,1,0:T(8,128)(2,1)S(1)} copy(bf16[512,16,32]{0,2,1:T(8,128)(2,1)S(1)} %bitcast.40) | data formatting | bytes 1048576 | tf_op jit(solution)/shard_map/reshape | solution.py:170
  106.5 4.8 %multiply_convert_fusion = bf16[512,16,128]{2,1,0:T(8,128)(2,1)} fusion(bf16[512,16,32]{2,1,0:T(8,128)(2,1)S(1)} %copy.20, bf16[512,32,128]{2,1,0:T(8,128)(2,1)} %bitcast.39), kind=kOutput, calls=%fused_computation.2 | convolution fusion | flops 69206016 | bytes 6815744 | tf_op jit(solution)/shard_map/bik,bkj->bij/dot_general | solution.py:171
  (1 shorter events, 0.0 us)
Async XLA Ops:
  6.5 81.3 %all-gather.2.cloned.1.call-start = ((), (), s32[]{:S(2)}) async-start(), calls=%async_computation | async-start | bytes 4456448 | tf_op jit(solution)/shard_map/all_gather | solution.py:156
  9.4 23.1 %copy-start = (s32[128]{0:T(128)S(1)}, s32[128]{0:T(128)}, u32[]{:S(2)}) copy-start(s32[128]{0:T(128)} %param.14) | copy-start | bytes 1540
  93.3 8.1 %copy-start.1 = (bf16[2,2,2]{0,2,1:T(2,128)(2,1)S(1)}, bf16[2,2,2]{0,2,1:T(2,128)(2,1)}, u32[]{:S(2)}) copy-start(bf16[2,2,2]{0,2,1:T(2,128)(2,1)} %constant.33.clone) | copy-start | bytes 52
Sparse Core Ops, SparseCore 0:
  32.6 55.1 all-gather.1
